TPU v7x, 128 devices: a whole 4x4x4 slice. The times are simulated.
128 devices in a mesh: req: 8 (over x, core), mlp: 16 (over y, z).
Axes of the slice: x: 4, y: 4, z: 4, core: 2. Of those that a mesh axis runs over, the one named last changes fastest.
Arguments:
- hidden_in: bfloat16 [16384, 2560], P(('req', 'mlp')), may hold values from -6 to 6
- queries: bfloat16 [16384, 2048], P(('req', 'mlp')), may hold values from -120 to 120
- keys_new: bfloat16 [16384, 512], P(('req', 'mlp')), may hold values from -4.4 to 4.4
- values_new: bfloat16 [16384, 512], P(('req', 'mlp')), may hold values from -5 to 5
- keys_cache: bfloat16 [4096, 512], P('req'), may hold values from -4.4 to 4.4
- values_cache: bfloat16 [4096, 512], P('req'), may hold values from -5 to 5
- out_weight: bfloat16 [2048, 2560], replicated, may hold values from -0.375 to 0.375
- norm_gain: float32 [2560], replicated, may hold values from 0.25 to 1.75
- gate_weight: bfloat16 [2560, 9728], P(None, 'mlp'), may hold values from -0.125 to 0.125
- up_weight: bfloat16 [2560, 9728], P(None, 'mlp'), may hold values from -0.125 to 0.125
- down_weight: bfloat16 [9728, 2560], P('mlp'), may hold values from -0.0625 to 0.0625
- lengths: int32 [8, 16], P('req', 'mlp'), may hold values from 1 to 128, 1536 in all within a row
- slot_request: int32 [128], replicated, may hold values from 0 to 127, each once
- cache_group: int32 [8, 4], replicated, may hold values from 0 to 3, each once within a row
Outputs:
- output: bfloat16 [16384, 2560], P(('req', 'mlp'))
Inputs may be any that keep to these rules, and one draw needn't show every extreme that they name: The 16 entries of one row of lengths sum to 1536, and one of them is 128. `slot_request`: each request appears in one slot. `cache_group`: each row names every group once.
All inputs are finite; a program needn't handle non-finite values. No bound on the sum of `lengths` on one device may be relied on, other than what follows from the above.
Results may differ from a plain program's by a relative error of at most 0.014.
Values may be sent and summed in bfloat16 or wider, within the bound.
No kernel may reach another device: no remote copies, remote signals or barrier semaphores. Data moves between devices by JAX's collectives and lax.ppermute only.
A program may use at most 128 MiB of HBM per device.

v0:
```python
import jax
import jax.numpy as jnp
from jax import lax
from jax.sharding import PartitionSpec as P

HEADS = 16
KVH = 4
HD = 128
GROUPS = 4
NEGATIVE = -1e30
EPSILON = 1e-06


def partial_attention(query_block, key_rows, value_rows, allowed):
    row_count = query_block.shape[0]
    key_count = key_rows.shape[0]
    per_group = HEADS // KVH
    query_heads = query_block.reshape(row_count, KVH, per_group, HD)
    key_heads = key_rows.reshape(key_count, KVH, HD)
    value_heads = value_rows.reshape(key_count, KVH, HD)
    scores = jnp.einsum(
        "tkgd,skd->kgts", query_heads, key_heads, preferred_element_type=jnp.float32
    ) * HD ** (-0.5)
    if allowed is not None:
        scores = jnp.where(allowed, scores, NEGATIVE)
    maxima = jnp.max(scores, axis=3)
    weights = jnp.exp(scores - maxima[..., None])
    totals = jnp.sum(weights, axis=3)
    context = jnp.einsum(
        "kgts,skd->tkgd",
        weights.astype(jnp.bfloat16),
        value_heads,
        preferred_element_type=jnp.float32,
    )
    context = context.reshape(row_count, HEADS * HD)
    maxima = jnp.transpose(maxima, (2, 0, 1)).reshape(row_count, HEADS)
    totals = jnp.transpose(totals, (2, 0, 1)).reshape(row_count, HEADS)
    return (context, maxima, totals)


def merge_pair(earlier, latest):
    context_early, maxima_early, totals_early = earlier
    context_late, maxima_late, totals_late = latest
    row_count = context_early.shape[0]
    highest = jnp.maximum(maxima_early, maxima_late)
    factor_early = jnp.exp(maxima_early - highest)
    factor_late = jnp.exp(maxima_late - highest)
    context = (
        context_early.reshape(row_count, HEADS, HD) * factor_early[..., None]
        + context_late.reshape(row_count, HEADS, HD) * factor_late[..., None]
    )
    return (
        context.reshape(row_count, HEADS * HD),
        highest,
        totals_early * factor_early + totals_late * factor_late,
    )


def shards(
    hidden_in,
    queries,
    keys_new,
    values_new,
    keys_cache,
    values_cache,
    out_weight,
    norm_gain,
    gate_weight,
    up_weight,
    down_weight,
    lengths,
    slot_request,
    cache_group,
):
    owners = lax.axis_size("req")
    columns = lax.axis_size("mlp")
    owner_index = lax.axis_index("req")
    column_index = lax.axis_index("mlp")
    tokens = queries.shape[0]
    width_kv = keys_cache.shape[1]
    piece_rows = keys_cache.shape[0] // GROUPS
    slot_group = slot_request // (slot_request.shape[0] // GROUPS)
    own_row = cache_group[owner_index]
    wanted = lax.dynamic_slice_in_dim(slot_group.reshape(owners, columns), column_index, 1, 1)[:, 0]
    group_ids = jnp.arange(GROUPS, dtype=jnp.int32)
    sub_block = jnp.sum(
        jnp.where(own_row[None, :] == wanted[:, None], group_ids[None, :], 0), axis=1
    )
    slab_keys = keys_cache.reshape(GROUPS, piece_rows, width_kv)
    slab_values = values_cache.reshape(GROUPS, piece_rows, width_kv)
    positions = jnp.arange(tokens, dtype=jnp.int32)
    causal = positions[:, None] >= positions[None, :]
    local_part = partial_attention(queries, keys_new, values_new, causal)
    send_keys = jnp.take(slab_keys, sub_block, axis=0)
    send_values = jnp.take(slab_values, sub_block, axis=0)
    got_keys, got_values = (
        lax.all_to_all(send_keys, "req", split_axis=0, concat_axis=0, tiled=True),
        lax.all_to_all(send_values, "req", split_axis=0, concat_axis=0, tiled=True),
    )
    prefix_part = partial_attention(
        queries,
        got_keys.reshape(owners * piece_rows, width_kv),
        got_values.reshape(owners * piece_rows, width_kv),
        None,
    )
    context, highest, totals = merge_pair(local_part, prefix_part)
    context = context.reshape(tokens, HEADS, HD)
    context = (context / totals[..., None]).reshape(tokens, HEADS * HD).astype(jnp.bfloat16)
    attended = jnp.dot(context, out_weight, preferred_element_type=jnp.float32)
    residual = (hidden_in.astype(jnp.float32) + attended).astype(jnp.bfloat16)
    widened = residual.astype(jnp.float32)
    normed = (
        widened
        * lax.rsqrt(jnp.mean(widened * widened, axis=1, keepdims=True) + EPSILON)
        * norm_gain[None, :]
    ).astype(jnp.bfloat16)
    shard_rows = lax.all_gather(normed, "mlp", axis=0, tiled=True)
    gate_values = jnp.dot(shard_rows, gate_weight, preferred_element_type=jnp.float32)
    upward = jnp.dot(shard_rows, up_weight, preferred_element_type=jnp.float32)
    hidden = (jax.nn.silu(gate_values) * upward).astype(jnp.bfloat16)
    partial_terms = jnp.dot(hidden, down_weight, preferred_element_type=jnp.float32)
    mixed = lax.psum_scatter(
        partial_terms.astype(jnp.bfloat16), "mlp", scatter_dimension=0, tiled=True
    ).astype(jnp.float32)
    result = residual.astype(jnp.float32) + mixed
    live_slot = positions[:, None] < lengths[0, 0]
    return jnp.where(live_slot, result, 0.0).astype(jnp.bfloat16)


def solution(mesh):
    return jax.shard_map(
        shards,
        mesh=mesh,
        in_specs=(
            P(("req", "mlp"), None),
            P(("req", "mlp"), None),
            P(("req", "mlp"), None),
            P(("req", "mlp"), None),
            P("req", None),
            P("req", None),
            P(),
            P(),
            P(None, "mlp"),
            P(None, "mlp"),
            P("mlp", None),
            P("req", "mlp"),
            P(),
            P(),
        ),
        out_specs=P(("req", "mlp"), None),
        check_vma=False,
    )
```

profile of v0, /device:TPU:0, one launch (start us, length us, event | category | flops | bytes accessed | tf_op | source)
XLA Modules:
  0.0 287.3 jit_solution(5620928909980571331)
XLA Ops:
  6.5 0.0 copy-start
  6.5 0.8 and_select_fusion
  7.4 0.1 reshape.109
  7.4 0.2 dynamic-slice_reduce_fusion
  7.6 0.9 dynamic-slice_reduce_fusion.1
  8.5 0.1 select_reduce_fusion
  8.6 2.6 gather_fusion
  11.2 0.0 copy-start.6
  11.2 0.0 copy-start.7
  11.2 2.7 gather_fusion.1
  13.9 3.1 %broadcast_select_fusion = (bf16[8,128,512]{2,1,0:T(8,128)(2,1)}, bf16[8,128,512]{2,1,0:T(8,128)(2,1)}) fusion(bf16[8,128,512]{2,1,0:T(8,128)(2,1)} %gather_fusion.1, pred[8]{0:T(512)(128)(4,1)S(1)} %compare_and_fusion, bf16[8,128,512]{2,1,0:T(8,128)(2,1)} %gather_fusion), kind=kLoop, calls=%fused_computation.31 | loop fusion | flops 1048576 | bytes 4194312 | tf_op jit(solution)/shard_map/jit(_take)/select_n | solution.py:95
  17.0 4.4 %all-to-all-start = ((bf16[8,128,512]{2,1,0:T(8,128)(2,1)}), bf16[8,128,512]{2,1,0:T(8,128)(2,1)}, u32[]{:S(2)}, u32[]{:S(2)}) async-start(bf16[8,128,512]{2,1,0:T(8,128)(2,1)} %get-tuple-element.10), calls=%async_computation | async-start | bytes 2097152 | tf_op jit(solution)/shard_map/all_to_all | solution.py:97
  21.4 2.2 reshape.105
  23.6 0.0 copy-done.6
  23.7 0.0 copy-done.7
  23.7 0.1 copy.55
  23.8 1.4 fusion.32
  25.2 0.2 fusion.18
  25.4 1.4 fusion.20
  26.8 10.7 %all-to-all-done = bf16[8,128,512]{2,1,0:T(8,128)(2,1)} async-done(((bf16[8,128,512]{2,1,0:T(8,128)(2,1)}), bf16[8,128,512]{2,1,0:T(8,128)(2,1)}, u32[]{:S(2)}, u32[]{:S(2)}) %all-to-all-start) | async-done | bytes 1048608 | tf_op jit(solution)/shard_map/all_to_all | solution.py:97
  37.5 4.2 %all-to-all-start.1 = ((bf16[8,128,512]{2,1,0:T(8,128)(2,1)}), bf16[8,128,512]{2,1,0:T(8,128)(2,1)}, u32[]{:S(2)}, u32[]{:S(2)}) async-start(bf16[8,128,512]{2,1,0:T(8,128)(2,1)} %get-tuple-element.9), calls=%async_computation.1 | async-start | bytes 2097152 | tf_op jit(solution)/shard_map/all_to_all | solution.py:98
  41.7 0.0 all-gather.2.cloned.1.call-start
  41.8 2.2 reshape.140
  44.0 2.6 bitcast_reduce_fusion
  46.6 0.0 copy-start.2
  46.6 3.2 %copy-done.2 = f32[4,1024,128,4]{2,1,3,0:T(8,128)} copy-done((f32[4,1024,128,4]{2,1,3,0:T(8,128)}, f32[4,1024,128,4]{2,1,3,0:T(8,128)S(1)}, u32[]{:S(2)}) %copy-start.2) | copy-done | bytes 8388632
  49.8 1.4 fusion.1
  51.3 6.4 %all-to-all-done.1 = bf16[8,128,512]{2,1,0:T(8,128)(2,1)} async-done(((bf16[8,128,512]{2,1,0:T(8,128)(2,1)}), bf16[8,128,512]{2,1,0:T(8,128)(2,1)}, u32[]{:S(2)}, u32[]{:S(2)}) %all-to-all-start.1) | async-done | bytes 1048608 | tf_op jit(solution)/shard_map/all_to_all | solution.py:98
  57.7 2.1 reshape.141
  59.8 0.0 copy-start.4
  59.8 0.0 copy-start.5
  59.8 5.4 %fusion.3 = f32[4,128,4,128]{3,1,2,0:T(8,128)S(1)} fusion(f32[4,1024,128,4]{2,1,3,0:T(8,128)} %copy-done.2, f32[4,4,128]{2,1,0:T(4,128)S(1)} %get-tuple-element.11, bf16[1024,4,128,1]{2,1,0,3:T(4,128)(2,1)} %bitcast.68), kind=kOutput, calls=%fused_computation.9 | convolution fusion | flops 543162368 | bytes 10493952 | tf_op jit(solution)/shard_map/kgts,skd->tkgd/dot_general | solution.py:29
  65.2 0.0 copy-done.4
  65.2 0.2 fusion.14
  65.4 0.0 copy-done.5
  65.4 0.0 copy-start.8
  65.5 5.6 %multiply_reduce_fusion = (f32[128]{0:T(128)S(1)}, f32[128,2560]{1,0:T(8,128)S(1)}) fusion(bf16[128,2048]{0,1:T(8,128)(2,1)S(1)} %fusion.14, bf16[2048,2560]{1,0:T(8,128)(2,1)} %param.22, bf16[128,2560]{1,0:T(8,128)(2,1)S(1)} %copy-done.5), kind=kOutput, calls=%fused_computation.21 | convolution fusion | flops 1344143232 | bytes 12976640 | tf_op jit(solution)/shard_map/dot_general | solution.py:109
  71.1 0.0 copy-start.3
  71.1 1.1 copy-done.3
  72.2 0.0 copy-done.8
  72.2 1.0 multiply_convert_fusion.1
  73.2 0.0 all-gather.2.cloned.1.call-update
  73.2 0.2 reduce-scatter.2.cloned.1.call-start
  73.4 80.9 %all-gather.2.cloned.1.call-done = bf16[2048,2560]{1,0:T(8,128)(2,1)} async-done(((bf16[128,2560]{1,0:T(8,128)(2,1)}), bf16[2048,2560]{1,0:T(8,128)(2,1)}) %all-gather.2.cloned.1.call-update) | async-done | bytes 10485776 | tf_op jit(solution)/shard_map/all_gather | solution.py:117
  154.3 11.7 %fusion.33 = f32[2048,608]{0,1:T(8,128)} fusion(bf16[2048,2560]{1,0:T(8,128)(2,1)} %all-gather.2.cloned.1.call-done, bf16[2560,608]{0,1:T(8,128)(2,1)} %param.24), kind=kOutput, calls=%fused_computation.61 | convolution fusion | flops 6375342080 | bytes 18579456 | tf_op jit(solution)/shard_map/dot_general | solution.py:118
  166.1 0.0 copy-done
  166.1 21.7 %convolution_convert_fusion = bf16[2048,2560]{1,0:T(8,128)(2,1)} fusion(bf16[608,2560]{1,0:T(8,128)(2,1)S(1)} %copy-done, f32[2048,608]{0,1:T(8,128)} %fusion.33, bf16[2048,2560]{1,0:T(8,128)(2,1)} %all-gather.2.cloned.1.call-done, bf16[2560,608]{0,1:T(8,128)(2,1)} %param.25), kind=kOutput, calls=%fused_computation.2 | convolution fusion | flops 12763398144 | bytes 32178176 | tf_op jit(solution)/shard_map/dot_general | solution.py:121
  187.8 0.0 copy-start.1
  187.8 0.0 reduce-scatter.2.cloned.1.call-update
  188.6 89.3 %reduce-scatter.2.cloned.1.call-done = bf16[128,2560]{1,0:T(8,128)(2,1)} async-done(((bf16[2048,2560]{1,0:T(8,128)(2,1)}), bf16[128,2560]{1,0:T(8,128)(2,1)}) %reduce-scatter.2.cloned.1.call-update) | async-done | bytes 655376 | tf_op jit(solution)/shard_map/reduce_scatter | solution.py:122
  278.0 2.5 select_convert_fusion
  280.5 0.0 copy-done.1
  (8 shorter events, 0.1 us)
Async XLA Ops:
  6.5 159.5 %copy-start = (bf16[608,2560]{1,0:T(8,128)(2,1)S(1)}, bf16[608,2560]{1,0:T(8,128)(2,1)}, u32[]{:S(2)}) copy-start(bf16[608,2560]{1,0:T(8,128)(2,1)} %param.26) | copy-start | bytes 9338884
  11.2 12.4 %copy-start.6 = (bf16[128,512]{1,0:T(8,128)(2,1)S(1)}, bf16[128,512]{1,0:T(8,128)(2,1)}, u32[]{:S(2)}) copy-start(bf16[128,512]{1,0:T(8,128)(2,1)} %param.18) | copy-start | bytes 393220
  11.2 12.4 %copy-start.7 = (bf16[128,512]{1,0:T(8,128)(2,1)S(1)}, bf16[128,512]{1,0:T(8,128)(2,1)}, u32[]{:S(2)}) copy-start(bf16[128,512]{1,0:T(8,128)(2,1)} %param.19) | copy-start | bytes 393220
  17.0 20.5 %all-to-all-start = ((bf16[8,128,512]{2,1,0:T(8,128)(2,1)}), bf16[8,128,512]{2,1,0:T(8,128)(2,1)}, u32[]{:S(2)}, u32[]{:S(2)}) async-start(bf16[8,128,512]{2,1,0:T(8,128)(2,1)} %get-tuple-element.10), calls=%async_computation | async-start | bytes 2097152 | tf_op jit(solution)/shard_map/all_to_all | solution.py:97
  37.5 20.2 %all-to-all-start.1 = ((bf16[8,128,512]{2,1,0:T(8,128)(2,1)}), bf16[8,128,512]{2,1,0:T(8,128)(2,1)}, u32[]{:S(2)}, u32[]{:S(2)}) async-start(bf16[8,128,512]{2,1,0:T(8,128)(2,1)} %get-tuple-element.9), calls=%async_computation.1 | async-start | bytes 2097152 | tf_op jit(solution)/shard_map/all_to_all | solution.py:98
  41.7 112.6 %all-gather.2.cloned.1.call-start = ((), (), s32[]{:S(2)}) async-start(), calls=%async_computation.3 | async-start | bytes 11141120 | tf_op jit(solution)/shard_map/all_gather | solution.py:117
  46.6 3.2 %copy-start.2 = (f32[4,1024,128,4]{2,1,3,0:T(8,128)}, f32[4,1024,128,4]{2,1,3,0:T(8,128)S(1)}, u32[]{:S(2)}) copy-start(f32[4,1024,128,4]{2,1,3,0:T(8,128)S(1)} %get-tuple-element.12) | copy-start | bytes 25165828
  59.8 5.4 %copy-start.4 = (f32[4,4,128,128]{2,3,1,0:T(8,128)S(1)}, f32[4,4,128,128]{2,3,1,0:T(8,128)}, u32[]{:S(2)}) copy-start(f32[4,4,128,128]{2,3,1,0:T(8,128)} %fusion.20) | copy-start | bytes 3145732
  59.8 5.6 %copy-start.5 = (bf16[128,2560]{1,0:T(8,128)(2,1)S(1)}, bf16[128,2560]{1,0:T(8,128)(2,1)}, u32[]{:S(2)}) copy-start(bf16[128,2560]{1,0:T(8,128)(2,1)} %param.16) | copy-start | bytes 1966084
  65.4 6.7 %copy-start.8 = (f32[2560]{0:T(1024)S(1)}, f32[2560]{0:T(1024)}, u32[]{:S(2)}) copy-start(f32[2560]{0:T(1024)} %param.23) | copy-start | bytes 30724
  71.1 1.1 copy-start.3
  73.2 204.7 %reduce-scatter.2.cloned.1.call-start = ((), (), s32[]{:S(2)}) async-start(), calls=%async_computation.4 | async-start | bytes 11141120 | tf_op jit(solution)/shard_map/reduce_scatter | solution.py:122
  187.8 92.7 %copy-start.1 = (bf16[608,2560]{1,0:T(8,128)(2,1)S(1)}, bf16[608,2560]{1,0:T(8,128)(2,1)}, u32[]{:S(2)}) copy-start(bf16[608,2560]{1,0:T(8,128)(2,1)} %param.26) | copy-start | bytes 9338884
Sparse Core Ops, SparseCore 0:
  73.3 80.9 all-gather.1
  187.9 89.9 reduce-scatter.1
where the time goes:
time: 288 us; the launch traced here: 287 us
  waiting for transfers between devices  187 us (65%)
  matrix products  49.9 us (17%)
  local copies, waits for them, and re-layouts  17.4 us (6%)
  between operations  14.3 us (5%)
  other arithmetic  9.37 us (3%)
  starting transfers between devices  8.92 us (3%)
    reduce_scatter x1, waiting for transfers between devices, shards(): lax.psum_scatter(partial_terms.astype(jnp.bfloat16), 'mlp', scatter_dimen...  89.3 us
    all_gather x1, waiting for transfers between devices, shards(): shard_rows = lax.all_gather(normed, 'mlp', axis=0, tiled=True)  80.9 us
    dot_general x1, matrix products, shards(): jnp.dot(hidden, down_weight, preferred_element_type=jnp.float32)  21.7 us
    dot_general x1, matrix products, shards(): jnp.dot(shard_rows, gate_weight, preferred_element_type=jnp.float32)  11.7 us
    all_to_all x1, waiting for transfers between devices, shards(): lax.all_to_all(send_keys, 'req', split_axis=0, concat_axis=0, tiled=True)  10.7 us
    dot_general x2, matrix products, partial_attention(): jnp.einsum('kgts,skd->tkgd', weights.astype(jnp.bfloat16), value_heads, p...  6.77 us
    all_to_all x1, waiting for transfers between devices, shards(): lax.all_to_all(send_values, 'req', split_axis=0, concat_axis=0, tiled=True)  6.41 us
  transfers between devices with their start and end apart: 4, of which 4 were waited for; matrix products, arithmetic and copies ran while one was open for 4% of the time, Pallas kernels for 0%

commit v1 on v0

--- a/solution.py
+++ b/solution.py
@@ -114,7 +114,22 @@
         * lax.rsqrt(jnp.mean(widened * widened, axis=1, keepdims=True) + EPSILON)
         * norm_gain[None, :]
     ).astype(jnp.bfloat16)
-    shard_rows = lax.all_gather(normed, "mlp", axis=0, tiled=True)
+    ways, here, step = (lax.axis_size("mlp"), lax.axis_index("mlp"), normed.shape[0])
+    lengths_2 = [n * ways if d == 0 else n for d, n in enumerate(normed.shape)]
+    shard_rows = lax.dynamic_update_slice_in_dim(
+        jnp.zeros(lengths_2, normed.dtype), normed, here * step, axis=0
+    )
+    going_up = going_down = normed
+    for far in range(1, ways // 2 + 1):
+        going_up = lax.ppermute(going_up, "mlp", [(d, (d + 1) % ways) for d in range(ways)])
+        shard_rows = lax.dynamic_update_slice_in_dim(
+            shard_rows, going_up, (here - far) % ways * step, axis=0
+        )
+        if 2 * far < ways:
+            going_down = lax.ppermute(going_down, "mlp", [(d, (d - 1) % ways) for d in range(ways)])
+            shard_rows = lax.dynamic_update_slice_in_dim(
+                shard_rows, going_down, (here + far) % ways * step, axis=0
+            )
     gate_values = jnp.dot(shard_rows, gate_weight, preferred_element_type=jnp.float32)
     upward = jnp.dot(shard_rows, up_weight, preferred_element_type=jnp.float32)
     hidden = (jax.nn.silu(gate_values) * upward).astype(jnp.bfloat16)

time: 288 us -> 343 us (1.19)
  starting transfers between devices: 8.92 us -> 47.2 us
  local copies, waits for them, and re-layouts: 17.4 us -> 36.4 us
    ppermute x0 -> x15, waiting for transfers between devices: none -> 83.1 us  [the longest x8 83.1 us: shards(): lax.ppermute(going_up, 'mlp', [(d, (d + 1) % ways) for d in range(ways)])]
    all_gather x1 -> x0, waiting for transfers between devices: 80.9 us -> none  [shards(): shard_rows = lax.all_gather(normed, 'mlp', axis=0, tiled=True)]
    ppermute x0 -> x15, starting transfers between devices: none -> 38.6 us  [the longest x7 36.6 us: shards(): lax.ppermute(going_down, 'mlp', [(d, (d - 1) % ways) for d in range(ways)])]
    dynamic_update_slice x0 -> x15, local copies, waits for them, and re-layouts: none -> 15.5 us  [the longest x8 8.22 us: shards(): lax.dynamic_update_slice_in_dim(shard_rows, going_up, (here - far) % ways...]
    broadcast_in_dim x0 -> x1, local copies, waits for them, and re-layouts: none -> 4.5 us  [shards(): jnp.zeros(lengths_2, normed.dtype)]
    reduce_scatter x1, waiting for transfers between devices: 89.3 us -> 85.5 us  [shards(): lax.psum_scatter(partial_terms.astype(jnp.bfloat16), 'mlp', scatter_dimen...]
  transfers between devices with their start and end apart: 4 -> 18, of which waited for: 4 -> 11; matrix products, arithmetic and copies ran while one was open for 4% -> 8% of each run, Pallas kernels for 0% -> 0%
where the time goes in v1:
time: 343 us; the launch traced here: 342 us
  waiting for transfers between devices  186 us (54%)
  matrix products  49 us (14%)
  starting transfers between devices  47.2 us (14%)
  local copies, waits for them, and re-layouts  36.4 us (11%)
  between operations  14.2 us (4%)
  other arithmetic  9.61 us (3%)
    reduce_scatter x1, waiting for transfers between devices, shards(): lax.psum_scatter(partial_terms.astype(jnp.bfloat16), 'mlp', scatter_dimen...  85.5 us
    ppermute x8, waiting for transfers between devices, shards(): lax.ppermute(going_up, 'mlp', [(d, (d + 1) % ways) for d in range(ways)])  83.1 us
    ppermute x7, starting transfers between devices, shards(): lax.ppermute(going_down, 'mlp', [(d, (d - 1) % ways) for d in range(ways)])  36.6 us
    dot_general x1, matrix products, shards(): jnp.dot(hidden, down_weight, preferred_element_type=jnp.float32)  21.7 us
    dot_general x1, matrix products, shards(): jnp.dot(shard_rows, gate_weight, preferred_element_type=jnp.float32)  10.9 us
    all_to_all x1, waiting for transfers between devices, shards(): lax.all_to_all(send_keys, 'req', split_axis=0, concat_axis=0, tiled=True)  10.7 us
    dynamic_update_slice x8, local copies, waits for them, and re-layouts, shards(): lax.dynamic_update_slice_in_dim(shard_rows, going_up, (here - far) % ways...  8.22 us
    dynamic_update_slice x7, local copies, waits for them, and re-layouts, shards(): lax.dynamic_update_slice_in_dim(shard_rows, going_down, (here + far) % wa...  7.31 us
  transfers between devices with their start and end apart: 18, of which 11 were waited for; matrix products, arithmetic and copies ran while one was open for 8% of the time, Pallas kernels for 0%

profile of v1, /device:TPU:0, one launch (start us, length us, event | category | flops | bytes accessed | tf_op | source)
XLA Modules:
  0.0 342.2 jit_solution(5613128402806919337)
XLA Ops:
  6.5 0.8 and_select_fusion
  7.4 0.1 reshape.109
  7.4 0.2 fusion.28
  7.6 0.9 fusion.29
  8.5 0.1 select_reduce_fusion
  8.6 2.6 gather_fusion
  11.3 2.6 gather_fusion.1
  13.9 3.1 broadcast_select_fusion
  17.0 4.4 %all-to-all-start = ((bf16[8,128,512]{2,1,0:T(8,128)(2,1)}), bf16[8,128,512]{2,1,0:T(8,128)(2,1)}, u32[]{:S(2)}, u32[]{:S(2)}) async-start(bf16[8,128,512]{2,1,0:T(8,128)(2,1)} %get-tuple-element.12), calls=%async_computation | async-start | bytes 2097152 | tf_op jit(solution)/shard_map/all_to_all | solution.py:97
  21.4 2.2 reshape.105
  23.6 0.1 copy.55
  23.8 1.4 fusion.34
  25.1 0.2 fusion.18
  25.3 1.4 fusion.20
  26.7 10.7 %all-to-all-done = bf16[8,128,512]{2,1,0:T(8,128)(2,1)} async-done(((bf16[8,128,512]{2,1,0:T(8,128)(2,1)}), bf16[8,128,512]{2,1,0:T(8,128)(2,1)}, u32[]{:S(2)}, u32[]{:S(2)}) %all-to-all-start) | async-done | bytes 1048608 | tf_op jit(solution)/shard_map/all_to_all | solution.py:97
  37.4 4.2 %all-to-all-start.1 = ((bf16[8,128,512]{2,1,0:T(8,128)(2,1)}), bf16[8,128,512]{2,1,0:T(8,128)(2,1)}, u32[]{:S(2)}, u32[]{:S(2)}) async-start(bf16[8,128,512]{2,1,0:T(8,128)(2,1)} %get-tuple-element.11), calls=%async_computation.1 | async-start | bytes 2097152 | tf_op jit(solution)/shard_map/all_to_all | solution.py:98
  41.7 0.0 reduce-scatter.2.cloned.1.call-start
  41.7 2.2 reshape.140
  43.9 2.6 bitcast_reduce_fusion
  46.6 3.2 copy-done.1
  49.8 1.4 fusion.1
  51.2 6.4 %all-to-all-done.1 = bf16[8,128,512]{2,1,0:T(8,128)(2,1)} async-done(((bf16[8,128,512]{2,1,0:T(8,128)(2,1)}), bf16[8,128,512]{2,1,0:T(8,128)(2,1)}, u32[]{:S(2)}, u32[]{:S(2)}) %all-to-all-start.1) | async-done | bytes 1048608 | tf_op jit(solution)/shard_map/all_to_all | solution.py:98
  57.6 2.2 reshape.141
  59.8 5.4 %fusion.3 = f32[4,128,4,128]{3,1,2,0:T(8,128)S(1)} fusion(f32[4,1024,128,4]{2,1,3,0:T(8,128)} %copy-done.1, f32[4,4,128]{2,1,0:T(4,128)S(1)} %get-tuple-element.13, bf16[1024,4,128,1]{2,1,0,3:T(4,128)(2,1)} %bitcast.68), kind=kOutput, calls=%fused_computation.9 | convolution fusion | flops 543162368 | bytes 10493952 | tf_op jit(solution)/shard_map/kgts,skd->tkgd/dot_general | solution.py:29
  65.2 0.2 fusion.14
  65.4 5.6 %multiply_reduce_fusion = (f32[128]{0:T(128)S(1)}, f32[128,2560]{1,0:T(8,128)S(1)}) fusion(bf16[128,2048]{0,1:T(8,128)(2,1)S(1)} %fusion.14, bf16[2048,2560]{1,0:T(8,128)(2,1)} %param.22, bf16[128,2560]{1,0:T(8,128)(2,1)S(1)} %copy-done.4), kind=kOutput, calls=%fused_computation.21 | convolution fusion | flops 1344143232 | bytes 12976640 | tf_op jit(solution)/shard_map/dot_general | solution.py:109
  71.1 4.5 %broadcast_in_dim.60 = bf16[2048,2560]{1,0:T(8,128)(2,1)} broadcast(bf16[]{:T(256)} %constant.137.clone.1), dimensions={} | broadcast | bytes 10485762 | tf_op jit(solution)/shard_map/broadcast_in_dim | solution.py:120
  75.6 1.3 constant_dynamic-update-slice_fusion.15
  76.8 1.9 collective-permute-start
  78.7 4.6 %collective-permute-start.1 = (bf16[128,2560]{1,0:T(8,128)(2,1)}, bf16[128,2560]{1,0:T(8,128)(2,1)}, u32[]{:S(2)}, u32[]{:S(2)}) collective-permute-start(bf16[128,2560]{1,0:T(8,128)(2,1)} %get-tuple-element.7), channel_id=1, source_target_pairs={{0,15},{1,0},{2,1},{3,2},{4,3},{5,4},{6,5},{7,6},{8,7},{9,8},{10,9... | collective-permute-start | bytes 1966088 | tf_op jit(solution)/shard_map/ppermute | solution.py:129
  83.3 14.7 %collective-permute-done = bf16[128,2560]{1,0:T(8,128)(2,1)} collective-permute-done((bf16[128,2560]{1,0:T(8,128)(2,1)}, bf16[128,2560]{1,0:T(8,128)(2,1)}, u32[]{:S(2)}, u32[]{:S(2)}) %collective-permute-start) | collective-permute-done | bytes 655392 | tf_op jit(solution)/shard_map/ppermute | solution.py:124
  98.1 5.3 %collective-permute-start.3 = (bf16[128,2560]{1,0:T(8,128)(2,1)}, bf16[128,2560]{1,0:T(8,128)(2,1)S(1)}, u32[]{:S(2)}, u32[]{:S(2)}) collective-permute-start(bf16[128,2560]{1,0:T(8,128)(2,1)} %collective-permute-done.1), channel_id=1, source_target_pairs={{0,15},{1,0},{2,1},{3,2},{4,3},{5,4},{6,5},{7,6},{8,7},{9,8},{10,9... | collective-permute-start | bytes 1966088 | tf_op jit(solution)/shard_map/ppermute | solution.py:129
  103.4 2.0 constant_dynamic-update-slice_fusion.14
  105.4 2.0 constant_dynamic-update-slice_fusion.13
  107.3 9.9 %collective-permute-done.2 = bf16[128,2560]{1,0:T(8,128)(2,1)S(1)} collective-permute-done((bf16[128,2560]{1,0:T(8,128)(2,1)}, bf16[128,2560]{1,0:T(8,128)(2,1)S(1)}, u32[]{:S(2)}, u32[]{:S(2)}) %collective-permute-start.2) | collective-permute-done | bytes 655392 | tf_op jit(solution)/shard_map/ppermute | solution.py:124
  117.2 5.3 %collective-permute-start.5 = (bf16[128,2560]{1,0:T(8,128)(2,1)S(1)}, bf16[128,2560]{1,0:T(8,128)(2,1)S(1)}, u32[]{:S(2)}, u32[]{:S(2)}) collective-permute-start(bf16[128,2560]{1,0:T(8,128)(2,1)S(1)} %collective-permute-done.3), channel_id=1, source_target_pairs={{0,15},{1,0},{2,1},{3,2},{4,3},{5,4},{6,5},{7,6},{8,7},{9,8},{10,9... | collective-permute-start | bytes 1966088 | tf_op jit(solution)/shard_map/ppermute | solution.py:129
  122.6 0.9 constant_dynamic-update-slice_fusion.12
  123.4 0.9 constant_dynamic-update-slice_fusion.11
  124.3 11.0 %collective-permute-done.4 = bf16[128,2560]{1,0:T(8,128)(2,1)S(1)} collective-permute-done((bf16[128,2560]{1,0:T(8,128)(2,1)S(1)}, bf16[128,2560]{1,0:T(8,128)(2,1)S(1)}, u32[]{:S(2)}, u32[]{:S(2)}) %collective-permute-start.4) | collective-permute-done | bytes 655392 | tf_op jit(solution)/shard_map/ppermute | solution.py:124
  135.3 5.3 %collective-permute-start.7 = (bf16[128,2560]{1,0:T(8,128)(2,1)S(1)}, bf16[128,2560]{1,0:T(8,128)(2,1)S(1)}, u32[]{:S(2)}, u32[]{:S(2)}) collective-permute-start(bf16[128,2560]{1,0:T(8,128)(2,1)S(1)} %collective-permute-done.5), channel_id=1, source_target_pairs={{0,15},{1,0},{2,1},{3,2},{4,3},{5,4},{6,5},{7,6},{8,7},{9,8},{10,9... | collective-permute-start | bytes 1966088 | tf_op jit(solution)/shard_map/ppermute | solution.py:129
  140.6 0.9 constant_dynamic-update-slice_fusion.10
  141.5 0.9 constant_dynamic-update-slice_fusion.9
  142.4 10.1 %collective-permute-done.6 = bf16[128,2560]{1,0:T(8,128)(2,1)S(1)} collective-permute-done((bf16[128,2560]{1,0:T(8,128)(2,1)S(1)}, bf16[128,2560]{1,0:T(8,128)(2,1)S(1)}, u32[]{:S(2)}, u32[]{:S(2)}) %collective-permute-start.6) | collective-permute-done | bytes 655392 | tf_op jit(solution)/shard_map/ppermute | solution.py:124
  152.5 5.3 %collective-permute-start.9 = (bf16[128,2560]{1,0:T(8,128)(2,1)S(1)}, bf16[128,2560]{1,0:T(8,128)(2,1)S(1)}, u32[]{:S(2)}, u32[]{:S(2)}) collective-permute-start(bf16[128,2560]{1,0:T(8,128)(2,1)S(1)} %collective-permute-done.7), channel_id=1, source_target_pairs={{0,15},{1,0},{2,1},{3,2},{4,3},{5,4},{6,5},{7,6},{8,7},{9,8},{10,9... | collective-permute-start | bytes 1966088 | tf_op jit(solution)/shard_map/ppermute | solution.py:129
  157.8 0.9 constant_dynamic-update-slice_fusion.8
  158.7 0.9 constant_dynamic-update-slice_fusion.7
  159.6 9.2 %collective-permute-done.8 = bf16[128,2560]{1,0:T(8,128)(2,1)S(1)} collective-permute-done((bf16[128,2560]{1,0:T(8,128)(2,1)S(1)}, bf16[128,2560]{1,0:T(8,128)(2,1)S(1)}, u32[]{:S(2)}, u32[]{:S(2)}) %collective-permute-start.8) | collective-permute-done | bytes 655392 | tf_op jit(solution)/shard_map/ppermute | solution.py:124
  168.9 5.3 %collective-permute-start.11 = (bf16[128,2560]{1,0:T(8,128)(2,1)S(1)}, bf16[128,2560]{1,0:T(8,128)(2,1)S(1)}, u32[]{:S(2)}, u32[]{:S(2)}) collective-permute-start(bf16[128,2560]{1,0:T(8,128)(2,1)S(1)} %collective-permute-done.9), channel_id=1, source_target_pairs={{0,15},{1,0},{2,1},{3,2},{4,3},{5,4},{6,5},{7,6},{8,7},{9,8},{10,9... | collective-permute-start | bytes 1966088 | tf_op jit(solution)/shard_map/ppermute | solution.py:129
  174.2 0.9 constant_dynamic-update-slice_fusion.6
  175.1 0.9 constant_dynamic-update-slice_fusion.5
  176.0 8.4 %collective-permute-done.10 = bf16[128,2560]{1,0:T(8,128)(2,1)S(1)} collective-permute-done((bf16[128,2560]{1,0:T(8,128)(2,1)S(1)}, bf16[128,2560]{1,0:T(8,128)(2,1)S(1)}, u32[]{:S(2)}, u32[]{:S(2)}) %collective-permute-start.10) | collective-permute-done | bytes 655392 | tf_op jit(solution)/shard_map/ppermute | solution.py:124
  184.4 5.3 %collective-permute-start.13 = (bf16[128,2560]{1,0:T(8,128)(2,1)S(1)}, bf16[128,2560]{1,0:T(8,128)(2,1)S(1)}, u32[]{:S(2)}, u32[]{:S(2)}) collective-permute-start(bf16[128,2560]{1,0:T(8,128)(2,1)S(1)} %collective-permute-done.11), channel_id=1, source_target_pairs={{0,15},{1,0},{2,1},{3,2},{4,3},{5,4},{6,5},{7,6},{8,7},{9,8},{10,9... | collective-permute-start | bytes 1966088 | tf_op jit(solution)/shard_map/ppermute | solution.py:129
  189.7 0.9 constant_dynamic-update-slice_fusion.4
  190.6 0.9 constant_dynamic-update-slice_fusion.3
  191.5 7.7 %collective-permute-done.12 = bf16[128,2560]{1,0:T(8,128)(2,1)S(1)} collective-permute-done((bf16[128,2560]{1,0:T(8,128)(2,1)S(1)}, bf16[128,2560]{1,0:T(8,128)(2,1)S(1)}, u32[]{:S(2)}, u32[]{:S(2)}) %collective-permute-start.12) | collective-permute-done | bytes 655392 | tf_op jit(solution)/shard_map/ppermute | solution.py:124
  199.2 0.9 constant_dynamic-update-slice_fusion.2
  200.1 0.9 constant_dynamic-update-slice_fusion.1
  201.0 12.1 %collective-permute-done.14 = bf16[128,2560]{1,0:T(8,128)(2,1)S(1)} collective-permute-done((bf16[128,2560]{1,0:T(8,128)(2,1)S(1)}, bf16[128,2560]{1,0:T(8,128)(2,1)S(1)}, u32[]{:S(2)}, u32[]{:S(2)}) %collective-permute-start.14) | collective-permute-done | bytes 655392 | tf_op jit(solution)/shard_map/ppermute | solution.py:124
  213.2 0.9 constant_dynamic-update-slice_fusion
  214.1 10.9 %fusion.37 = f32[2048,608]{0,1:T(8,128)} fusion(bf16[2048,2560]{1,0:T(8,128)(2,1)} %constant_dynamic-update-slice_fusion, bf16[2560,608]{0,1:T(8,128)(2,1)S(1)} %copy-done.8), kind=kOutput, calls=%fused_computation.80 | convolution fusion | flops 6375342080 | bytes 18579456 | tf_op jit(solution)/shard_map/dot_general | solution.py:133
  225.0 21.7 %convolution_convert_fusion = bf16[2048,2560]{1,0:T(8,128)(2,1)} fusion(bf16[608,2560]{1,0:T(8,128)(2,1)S(1)} %copy-done, f32[2048,608]{0,1:T(8,128)} %fusion.37, bf16[2048,2560]{1,0:T(8,128)(2,1)} %constant_dynamic-update-slice_fusion, bf16[2560,608]{0,1:T(8,128)(2,1)} %param.25), kind=kOutput, calls=%fused_computation.2 | convolution fusion | flops 12763398144 | bytes 32178176 | tf_op jit(solution)/shard_map/dot_general | solution.py:136
  246.7 0.0 reduce-scatter.2.cloned.1.call-update
  247.3 85.5 %reduce-scatter.2.cloned.1.call-done = bf16[128,2560]{1,0:T(8,128)(2,1)} async-done(((bf16[2048,2560]{1,0:T(8,128)(2,1)}), bf16[128,2560]{1,0:T(8,128)(2,1)}) %reduce-scatter.2.cloned.1.call-update) | async-done | bytes 655376 | tf_op jit(solution)/shard_map/reduce_scatter | solution.py:137
  332.8 2.5 select_convert_fusion
  (39 shorter events, 0.2 us)
Async XLA Ops:
  6.5 218.4 %copy-start = (bf16[608,2560]{1,0:T(8,128)(2,1)S(1)}, bf16[608,2560]{1,0:T(8,128)(2,1)}, u32[]{:S(2)}) copy-start(bf16[608,2560]{1,0:T(8,128)(2,1)} %param.26) | copy-start | bytes 9338884
  6.5 17.0 %copy-start.5 = (bf16[128,512]{1,0:T(8,128)(2,1)S(1)}, bf16[128,512]{1,0:T(8,128)(2,1)}, u32[]{:S(2)}) copy-start(bf16[128,512]{1,0:T(8,128)(2,1)} %param.18) | copy-start | bytes 393220
  6.5 17.1 %copy-start.6 = (bf16[128,512]{1,0:T(8,128)(2,1)S(1)}, bf16[128,512]{1,0:T(8,128)(2,1)}, u32[]{:S(2)}) copy-start(bf16[128,512]{1,0:T(8,128)(2,1)} %param.19) | copy-start | bytes 393220
  17.0 20.5 %all-to-all-start = ((bf16[8,128,512]{2,1,0:T(8,128)(2,1)}), bf16[8,128,512]{2,1,0:T(8,128)(2,1)}, u32[]{:S(2)}, u32[]{:S(2)}) async-start(bf16[8,128,512]{2,1,0:T(8,128)(2,1)} %get-tuple-element.12), calls=%async_computation | async-start | bytes 2097152 | tf_op jit(solution)/shard_map/all_to_all | solution.py:97
  37.4 20.2 %all-to-all-start.1 = ((bf16[8,128,512]{2,1,0:T(8,128)(2,1)}), bf16[8,128,512]{2,1,0:T(8,128)(2,1)}, u32[]{:S(2)}, u32[]{:S(2)}) async-start(bf16[8,128,512]{2,1,0:T(8,128)(2,1)} %get-tuple-element.11), calls=%async_computation.1 | async-start | bytes 2097152 | tf_op jit(solution)/shard_map/all_to_all | solution.py:98
  41.7 291.2 %reduce-scatter.2.cloned.1.call-start = ((), (), s32[]{:S(2)}) async-start(), calls=%async_computation.3 | async-start | bytes 11141120 | tf_op jit(solution)/shard_map/reduce_scatter | solution.py:137
  46.5 3.2 copy-start.1
  59.8 5.4 %copy-start.3 = (f32[4,4,128,128]{2,3,1,0:T(8,128)S(1)}, f32[4,4,128,128]{2,3,1,0:T(8,128)}, u32[]{:S(2)}) copy-start(f32[4,4,128,128]{2,3,1,0:T(8,128)} %fusion.20) | copy-start | bytes 3145732
  59.8 5.6 %copy-start.4 = (bf16[128,2560]{1,0:T(8,128)(2,1)S(1)}, bf16[128,2560]{1,0:T(8,128)(2,1)}, u32[]{:S(2)}) copy-start(bf16[128,2560]{1,0:T(8,128)(2,1)} %param.16) | copy-start | bytes 1966084
  65.4 10.2 %copy-start.7 = (f32[2560]{0:T(1024)S(1)}, f32[2560]{0:T(1024)}, u32[]{:S(2)}) copy-start(f32[2560]{0:T(1024)} %param.23) | copy-start | bytes 30724
  71.0 4.5 %copy-start.2 = (f32[128,2560]{1,0:T(8,128)}, f32[128,2560]{1,0:T(8,128)S(1)}, u32[]{:S(2)}) copy-start(f32[128,2560]{1,0:T(8,128)S(1)} %get-tuple-element.18) | copy-start | bytes 3932164
  76.8 21.2 %collective-permute-start = (bf16[128,2560]{1,0:T(8,128)(2,1)}, bf16[128,2560]{1,0:T(8,128)(2,1)}, u32[]{:S(2)}, u32[]{:S(2)}) collective-permute-start(bf16[128,2560]{1,0:T(8,128)(2,1)} %get-tuple-element.7), channel_id=1, source_target_pairs={{0,1},{1,2},{2,3},{3,4},{4,5},{5,6},{6,7},{7,8},{8,9},{9,10},{10,1... | collective-permute-start | bytes 1966088 | tf_op jit(solution)/shard_map/ppermute | solution.py:124
  78.7 19.3 %collective-permute-start.1 = (bf16[128,2560]{1,0:T(8,128)(2,1)}, bf16[128,2560]{1,0:T(8,128)(2,1)}, u32[]{:S(2)}, u32[]{:S(2)}) collective-permute-start(bf16[128,2560]{1,0:T(8,128)(2,1)} %get-tuple-element.7), channel_id=1, source_target_pairs={{0,15},{1,0},{2,1},{3,2},{4,3},{5,4},{6,5},{7,6},{8,7},{9,8},{10,9... | collective-permute-start | bytes 1966088 | tf_op jit(solution)/shard_map/ppermute | solution.py:129
  83.3 130.8 %copy-start.8 = (bf16[2560,608]{0,1:T(8,128)(2,1)S(1)}, bf16[2560,608]{0,1:T(8,128)(2,1)}, u32[]{:S(2)}) copy-start(bf16[2560,608]{0,1:T(8,128)(2,1)} %param.24) | copy-start | bytes 9338884
  98.1 19.1 %collective-permute-start.2 = (bf16[128,2560]{1,0:T(8,128)(2,1)}, bf16[128,2560]{1,0:T(8,128)(2,1)S(1)}, u32[]{:S(2)}, u32[]{:S(2)}) collective-permute-start(bf16[128,2560]{1,0:T(8,128)(2,1)} %collective-permute-done), channel_id=1, source_target_pairs={{0,1},{1,2},{2,3},{3,4},{4,5},{5,6},{6,7},{7,8},{8,9},{9,10},{10,1... | collective-permute-start | bytes 1966088 | tf_op jit(solution)/shard_map/ppermute | solution.py:124
  98.1 19.1 %collective-permute-start.3 = (bf16[128,2560]{1,0:T(8,128)(2,1)}, bf16[128,2560]{1,0:T(8,128)(2,1)S(1)}, u32[]{:S(2)}, u32[]{:S(2)}) collective-permute-start(bf16[128,2560]{1,0:T(8,128)(2,1)} %collective-permute-done.1), channel_id=1, source_target_pairs={{0,15},{1,0},{2,1},{3,2},{4,3},{5,4},{6,5},{7,6},{8,7},{9,8},{10,9... | collective-permute-start | bytes 1966088 | tf_op jit(solution)/shard_map/ppermute | solution.py:129
  117.2 18.1 %collective-permute-start.4 = (bf16[128,2560]{1,0:T(8,128)(2,1)S(1)}, bf16[128,2560]{1,0:T(8,128)(2,1)S(1)}, u32[]{:S(2)}, u32[]{:S(2)}) collective-permute-start(bf16[128,2560]{1,0:T(8,128)(2,1)S(1)} %collective-permute-done.2), channel_id=1, source_target_pairs={{0,1},{1,2},{2,3},{3,4},{4,5},{5,6},{6,7},{7,8},{8,9},{9,10},{10,1... | collective-permute-start | bytes 1966088 | tf_op jit(solution)/shard_map/ppermute | solution.py:124
  117.2 18.1 %collective-permute-start.5 = (bf16[128,2560]{1,0:T(8,128)(2,1)S(1)}, bf16[128,2560]{1,0:T(8,128)(2,1)S(1)}, u32[]{:S(2)}, u32[]{:S(2)}) collective-permute-start(bf16[128,2560]{1,0:T(8,128)(2,1)S(1)} %collective-permute-done.3), channel_id=1, source_target_pairs={{0,15},{1,0},{2,1},{3,2},{4,3},{5,4},{6,5},{7,6},{8,7},{9,8},{10,9... | collective-permute-start | bytes 1966088 | tf_op jit(solution)/shard_map/ppermute | solution.py:129
  135.3 17.2 %collective-permute-start.6 = (bf16[128,2560]{1,0:T(8,128)(2,1)S(1)}, bf16[128,2560]{1,0:T(8,128)(2,1)S(1)}, u32[]{:S(2)}, u32[]{:S(2)}) collective-permute-start(bf16[128,2560]{1,0:T(8,128)(2,1)S(1)} %collective-permute-done.4), channel_id=1, source_target_pairs={{0,1},{1,2},{2,3},{3,4},{4,5},{5,6},{6,7},{7,8},{8,9},{9,10},{10,1... | collective-permute-start | bytes 1966088 | tf_op jit(solution)/shard_map/ppermute | solution.py:124
  135.3 17.2 %collective-permute-start.7 = (bf16[128,2560]{1,0:T(8,128)(2,1)S(1)}, bf16[128,2560]{1,0:T(8,128)(2,1)S(1)}, u32[]{:S(2)}, u32[]{:S(2)}) collective-permute-start(bf16[128,2560]{1,0:T(8,128)(2,1)S(1)} %collective-permute-done.5), channel_id=1, source_target_pairs={{0,15},{1,0},{2,1},{3,2},{4,3},{5,4},{6,5},{7,6},{8,7},{9,8},{10,9... | collective-permute-start | bytes 1966088 | tf_op jit(solution)/shard_map/ppermute | solution.py:129
  152.5 16.4 %collective-permute-start.8 = (bf16[128,2560]{1,0:T(8,128)(2,1)S(1)}, bf16[128,2560]{1,0:T(8,128)(2,1)S(1)}, u32[]{:S(2)}, u32[]{:S(2)}) collective-permute-start(bf16[128,2560]{1,0:T(8,128)(2,1)S(1)} %collective-permute-done.6), channel_id=1, source_target_pairs={{0,1},{1,2},{2,3},{3,4},{4,5},{5,6},{6,7},{7,8},{8,9},{9,10},{10,1... | collective-permute-start | bytes 1966088 | tf_op jit(solution)/shard_map/ppermute | solution.py:124
  152.5 16.4 %collective-permute-start.9 = (bf16[128,2560]{1,0:T(8,128)(2,1)S(1)}, bf16[128,2560]{1,0:T(8,128)(2,1)S(1)}, u32[]{:S(2)}, u32[]{:S(2)}) collective-permute-start(bf16[128,2560]{1,0:T(8,128)(2,1)S(1)} %collective-permute-done.7), channel_id=1, source_target_pairs={{0,15},{1,0},{2,1},{3,2},{4,3},{5,4},{6,5},{7,6},{8,7},{9,8},{10,9... | collective-permute-start | bytes 1966088 | tf_op jit(solution)/shard_map/ppermute | solution.py:129
  168.8 15.5 %collective-permute-start.10 = (bf16[128,2560]{1,0:T(8,128)(2,1)S(1)}, bf16[128,2560]{1,0:T(8,128)(2,1)S(1)}, u32[]{:S(2)}, u32[]{:S(2)}) collective-permute-start(bf16[128,2560]{1,0:T(8,128)(2,1)S(1)} %collective-permute-done.8), channel_id=1, source_target_pairs={{0,1},{1,2},{2,3},{3,4},{4,5},{5,6},{6,7},{7,8},{8,9},{9,10},{10,1... | collective-permute-start | bytes 1966088 | tf_op jit(solution)/shard_map/ppermute | solution.py:124
  168.9 15.5 %collective-permute-start.11 = (bf16[128,2560]{1,0:T(8,128)(2,1)S(1)}, bf16[128,2560]{1,0:T(8,128)(2,1)S(1)}, u32[]{:S(2)}, u32[]{:S(2)}) collective-permute-start(bf16[128,2560]{1,0:T(8,128)(2,1)S(1)} %collective-permute-done.9), channel_id=1, source_target_pairs={{0,15},{1,0},{2,1},{3,2},{4,3},{5,4},{6,5},{7,6},{8,7},{9,8},{10,9... | collective-permute-start | bytes 1966088 | tf_op jit(solution)/shard_map/ppermute | solution.py:129
  184.4 14.9 %collective-permute-start.12 = (bf16[128,2560]{1,0:T(8,128)(2,1)S(1)}, bf16[128,2560]{1,0:T(8,128)(2,1)S(1)}, u32[]{:S(2)}, u32[]{:S(2)}) collective-permute-start(bf16[128,2560]{1,0:T(8,128)(2,1)S(1)} %collective-permute-done.10), channel_id=1, source_target_pairs={{0,1},{1,2},{2,3},{3,4},{4,5},{5,6},{6,7},{7,8},{8,9},{9,10},{10,1... | collective-permute-start | bytes 1966088 | tf_op jit(solution)/shard_map/ppermute | solution.py:124
  184.4 15.8 %collective-permute-start.13 = (bf16[128,2560]{1,0:T(8,128)(2,1)S(1)}, bf16[128,2560]{1,0:T(8,128)(2,1)S(1)}, u32[]{:S(2)}, u32[]{:S(2)}) collective-permute-start(bf16[128,2560]{1,0:T(8,128)(2,1)S(1)} %collective-permute-done.11), channel_id=1, source_target_pairs={{0,15},{1,0},{2,1},{3,2},{4,3},{5,4},{6,5},{7,6},{8,7},{9,8},{10,9... | collective-permute-start | bytes 1966088 | tf_op jit(solution)/shard_map/ppermute | solution.py:129
  199.2 13.9 %collective-permute-start.14 = (bf16[128,2560]{1,0:T(8,128)(2,1)S(1)}, bf16[128,2560]{1,0:T(8,128)(2,1)S(1)}, u32[]{:S(2)}, u32[]{:S(2)}) collective-permute-start(bf16[128,2560]{1,0:T(8,128)(2,1)S(1)} %collective-permute-done.12), channel_id=1, source_target_pairs={{0,1},{1,2},{2,3},{3,4},{4,5},{5,6},{6,7},{7,8},{8,9},{9,10},{10,1... | collective-permute-start | bytes 1966088 | tf_op jit(solution)/shard_map/ppermute | solution.py:124
Sparse Core Ops, SparseCore 0:
  246.8 85.9 reduce-scatter.1
